TPU v7x, 512 devices: a whole 4x4x16 slice. The times are simulated.
512 devices in a mesh: req: 128 (over z, x, core), head: 4 (over y).
Axes of the slice: x: 4, y: 4, z: 16, core: 2. Of those that a mesh axis runs over, the one named last changes fastest.
Arguments:
- query_proj: bfloat16 [32768, 2048], P('req', 'head'), may hold values from -6 to 6
- key_proj: bfloat16 [32768, 2048], P('req', 'head'), may hold values from -6 to 6
- value_proj: bfloat16 [32768, 2048], P('req', 'head'), may hold values from -6 to 6
- lengths: int32 [64], replicated, may hold values from 1 to 8, 256 in all
- page_table: int32 [256], P('req'), may hold values from 0 to 255, as said below
- out_weight: bfloat16 [2048, 4096], P('req', 'head'), may hold values from -0.125 to 0.125
- out_bias: float32 [4096], P('head'), may hold values from -3 to 3
Outputs:
- attended: bfloat16 [32768, 4096], P('req', 'head')
- kv_pages: bfloat16 [256, 2, 128, 2048], P('req', None, None, 'head')
Inputs may be any that keep to these rules, and one draw needn't show every extreme that they name: page_table is a permutation in which page b of the stream goes to one of the pages 2 * (b // 2) to 2 * (b // 2) + 1.
All inputs are finite; a program needn't handle non-finite values.
Results may differ from a plain program's by a relative error of at most 0.0046.
Values may be sent and summed in bfloat16 or wider, within the bound.
No kernel may reach another device: no remote copies, remote signals or barrier semaphores. Data moves between devices by JAX's collectives and lax.ppermute only.
A program may use at most 64 MiB of HBM per device.

v0:
```python
import math
import jax
import jax.numpy as jnp
from jax import lax
from jax.sharding import PartitionSpec as P

DH = 128
ROT = 32
PAGE = 128
BLK_DEV = 2
REACH = 4
TOK_DEV = 256
rope_base = 10000.0


def passed_along(array, axis, by):
    count = lax.axis_size(axis)
    pairs = [(i, i + by) for i in range(count) if 0 <= i + by < count]
    return lax.ppermute(array, axis, pairs)


def request_info(lengths, token_index):
    request_ends = jnp.cumsum(lengths) * PAGE
    request_starts = request_ends - lengths * PAGE
    inside = request_starts[None, :] <= token_index[:, None]
    request_id = jnp.sum(inside.astype(jnp.int32), axis=1) - 1
    opening = jnp.max(jnp.where(inside, request_starts[None, :], 0), axis=1)
    return (request_id, token_index - opening)


def rotate_heads(projected, position):
    values_f32 = projected.astype(jnp.float32)
    half_rot = ROT // 2
    frequency = jnp.exp(
        jnp.arange(half_rot, dtype=jnp.float32) * (-2.0 * math.log(rope_base) / ROT)
    )
    angles = position.astype(jnp.float32)[:, None] * frequency[None, :]
    cosine = jnp.cos(angles)[:, None, :]
    sine = jnp.sin(angles)[:, None, :]
    front_half = values_f32[..., :half_rot]
    back_half = values_f32[..., half_rot:ROT]
    turned = jnp.concatenate(
        [
            front_half * cosine - back_half * sine,
            back_half * cosine + front_half * sine,
            values_f32[..., ROT:],
        ],
        axis=-1,
    )
    return turned.astype(jnp.bfloat16)


def attend_block(query_rot, key_rot, value_rows, query_id, query_token, key_id, key_token):
    scores = jnp.einsum("qhd,khd->hqk", query_rot, key_rot, preferred_element_type=jnp.float32) * (
        1.0 / math.sqrt(DH)
    )
    allowed = (query_id[:, None] == key_id[None, :]) & (key_token[None, :] <= query_token[:, None])
    scores = jnp.where(allowed[None], scores, -jnp.inf)
    row_max = jnp.max(scores, axis=-1, keepdims=True)
    raised = jnp.exp(scores - row_max)
    probs = (raised / jnp.sum(raised, axis=-1, keepdims=True)).astype(jnp.bfloat16)
    mixed = jnp.einsum("hqk,khd->qhd", probs, value_rows, preferred_element_type=jnp.float32)
    return mixed.astype(jnp.bfloat16)


def local(query_proj, key_proj, value_proj, lengths, page_table, out_weight, out_bias):
    local_heads = query_proj.shape[1] // DH
    device_rank = lax.axis_index("req")
    first_token = device_rank * TOK_DEV
    own_tokens = first_token + jnp.arange(TOK_DEV, dtype=jnp.int32)
    request_id, position = request_info(lengths, own_tokens)
    query_rot = rotate_heads(query_proj.reshape(TOK_DEV, local_heads, DH), position)
    key_flat = rotate_heads(key_proj.reshape(TOK_DEV, local_heads, DH), position).reshape(
        TOK_DEV, local_heads * DH
    )
    key_list = [key_flat]
    value_list = [value_proj]
    for distance in range(1, REACH + 1):
        far_key, far_value = passed_along((key_flat, value_proj), "req", distance)
        key_list.append(far_key)
        value_list.append(far_value)
    key_stack = jnp.stack(key_list[::-1], axis=0)
    value_stack = jnp.stack(value_list[::-1], axis=0)
    key_rows = (REACH + 1) * TOK_DEV
    key_all = key_stack.reshape(key_rows, local_heads, DH)
    value_all = value_stack.reshape(key_rows, local_heads, DH)
    key_tokens = first_token - REACH * TOK_DEV + jnp.arange(key_rows, dtype=jnp.int32)
    key_id, key_position = request_info(lengths, key_tokens)
    mixed = attend_block(query_rot, key_all, value_all, request_id, own_tokens, key_id, key_tokens)
    heads_out = mixed.reshape(TOK_DEV, local_heads * DH)
    weight_all_rows = lax.all_gather(out_weight, "req", axis=0, tiled=True)
    weight_own_rows = lax.all_to_all(
        weight_all_rows, "head", split_axis=0, concat_axis=1, tiled=True
    )
    partial_value = jnp.dot(heads_out, weight_own_rows, preferred_element_type=jnp.float32)
    summed = lax.psum_scatter(partial_value, "head", scatter_dimension=1, tiled=True)
    attended = (summed + out_bias).astype(jnp.bfloat16)
    local_page = page_table - device_rank * BLK_DEV
    picker = (local_page[:, None] == jnp.arange(BLK_DEV, dtype=jnp.int32)[None, :]).astype(
        jnp.bfloat16
    )
    page_blocks = jnp.stack(
        [
            key_flat.reshape(BLK_DEV, PAGE, local_heads * DH),
            value_proj.reshape(BLK_DEV, PAGE, local_heads * DH),
        ],
        axis=1,
    )
    kv_pages = jnp.einsum(
        "bp,bctd->pctd", picker, page_blocks, preferred_element_type=jnp.float32
    ).astype(jnp.bfloat16)
    return (attended, kv_pages)


def solution(mesh):
    placed = (
        P("req", "head"),
        P("req", "head"),
        P("req", "head"),
        P(),
        P("req"),
        P("req", "head"),
        P("head"),
    )
    return jax.shard_map(
        local,
        mesh=mesh,
        in_specs=placed,
        out_specs=(P("req", "head"), P("req", None, None, "head")),
        check_vma=False,
    )
```

profile of v0, /device:TPU:1, one launch (start us, length us, event | category | flops | bytes accessed | tf_op | source)
XLA Modules:
  0.0 291.5 jit_solution(7986303135102277170)
XLA Ops:
  7.2 0.0 all-gather.2.cloned.1.call-start
  7.2 0.7 all-gather.2.cloned.1.call-update
  7.9 0.7 copy.62
  8.6 0.1 reduce-window.9
  8.8 0.1 multiply_reduce_fusion
  8.9 0.7 multiply_subtract_fusion.1
  9.5 0.1 fusion.11
  9.6 0.1 multiply_cosine_fusion
  9.8 0.1 copy.65
  9.9 0.1 copy.66
  10.0 1.1 copy.68
  11.1 0.2 copy.84
  11.3 0.2 copy.85
  11.5 0.0 copy-start.2
  11.6 0.0 copy-start.4
  11.6 0.1 multiply_subtract_fusion
  11.7 0.1 copy.71
  11.8 0.1 copy.72
  12.0 6.2 %collective-permute-start.4 = (bf16[256,512]{0,1:T(8,128)(2,1)S(1)}, bf16[256,512]{0,1:T(8,128)(2,1)}, u32[]{:S(2)}, u32[]{:S(2)}) collective-permute-start(bf16[256,512]{0,1:T(8,128)(2,1)S(1)} %bitcast.44), channel_id=1, source_target_pairs={{0,16},{4,20},{8,24},{12,28},{16,32},{20,36},{24,40},{28,44},{32,4... | collective-permute-start | bytes 786440 | tf_op jit(solution)/shard_map/ppermute | solution.py:19
  18.2 4.3 %collective-permute-start.5 = (bf16[256,512]{0,1:T(8,128)(2,1)S(1)}, bf16[256,512]{0,1:T(8,128)(2,1)}, u32[]{:S(2)}, u32[]{:S(2)}) collective-permute-start(bf16[256,512]{0,1:T(8,128)(2,1)S(1)} %bitcast.45), channel_id=1, source_target_pairs={{0,12},{4,16},{8,20},{12,24},{16,28},{20,32},{24,36},{28,40},{32,4... | collective-permute-start | bytes 786440 | tf_op jit(solution)/shard_map/ppermute | solution.py:19
  22.5 2.4 collective-permute-start.6
  24.9 1.9 collective-permute-start.7
  26.9 5.3 %collective-permute-start = (bf16[256,512]{1,0:T(8,128)(2,1)S(1)}, bf16[256,512]{1,0:T(8,128)(2,1)}, u32[]{:S(2)}, u32[]{:S(2)}) collective-permute-start(bf16[256,512]{1,0:T(8,128)(2,1)S(1)} %copy-done.2), channel_id=1, source_target_pairs={{0,16},{4,20},{8,24},{12,28},{16,32},{20,36},{24,40},{28,44},{32,4... | collective-permute-start | bytes 786440 | tf_op jit(solution)/shard_map/ppermute | solution.py:19
  32.2 0.1 copy.63
  32.3 0.2 copy.64
  32.6 0.1 convert_reduce_fusion
  32.7 0.3 compare_and_fusion
  33.1 135.1 %all-gather.2.cloned.1.call-done = bf16[2048,1024]{1,0:T(8,128)(2,1)} async-done(((bf16[16,1024]{1,0:T(8,128)(2,1)}), bf16[2048,1024]{1,0:T(8,128)(2,1)}) %all-gather.2.cloned.1.call-update) | async-done | bytes 4194320 | tf_op jit(solution)/shard_map/all_gather | solution.py:91
  168.1 4.8 %all-to-all-start = ((bf16[4,512,1024]{2,1,0:T(8,128)(2,1)}), bf16[4,512,1024]{2,1,0:T(8,128)(2,1)}, u32[]{:S(2)}, u32[]{:S(2)}) async-start(bf16[4,512,1024]{2,1,0:T(8,128)(2,1)} %bitcast.43), calls=%async_computation | async-start | bytes 8388608 | tf_op jit(solution)/shard_map/all_to_all | solution.py:92
  172.9 0.0 reduce-scatter.2.cloned.1.call-start
  173.0 0.3 subtract_convert_fusion
  173.3 0.1 slice.27
  173.4 1.0 pad_maximum_fusion.2
  174.4 0.0 collective-permute-done.4
  174.4 3.7 %collective-permute-start.1 = (bf16[256,512]{1,0:T(8,128)(2,1)S(1)}, bf16[256,512]{1,0:T(8,128)(2,1)S(1)}, u32[]{:S(2)}, u32[]{:S(2)}) collective-permute-start(bf16[256,512]{1,0:T(8,128)(2,1)S(1)} %copy-done.2), channel_id=1, source_target_pairs={{0,12},{4,16},{8,20},{12,24},{16,28},{20,32},{24,36},{28,40},{32,4... | collective-permute-start | bytes 786440 | tf_op jit(solution)/shard_map/ppermute | solution.py:19
  178.0 1.7 bitcast_dynamic-update-slice_fusion.3
  179.7 2.5 collective-permute-start.2
  182.3 1.0 bitcast_dynamic-update-slice_fusion.8
  183.2 1.9 collective-permute-start.3
  185.2 1.7 bitcast_dynamic-update-slice_fusion.2
  186.8 0.7 bitcast_dynamic-update-slice_fusion.1
  187.6 0.7 bitcast_dynamic-update-slice_fusion
  188.3 0.7 constant_dynamic-update-slice_fusion
  189.1 1.6 copy.73
  190.7 1.3 reshape.211
  192.0 1.0 bitcast_dynamic-update-slice_fusion.6
  193.0 1.0 bitcast_dynamic-update-slice_fusion.5
  194.0 1.3 reshape.209
  195.2 0.5 copy-done
  195.8 3.1 %exponential_reduce_fusion = f32[4,256]{1,0:T(4,128)S(1)} fusion(bf16[256,4,128]{2,0,1:T(8,128)(2,1)} %pad_maximum_fusion.2, pred[256,1280]{1,0:T(8,128)(4,1)S(1)} %compare_and_fusion, bf16[1280,4,128]{2,1,0:T(4,128)(2,1)S(1)} %copy-done), kind=kOutput, calls=%fused_computation.4 | convolution fusion | flops 340788480 | bytes 1904640 | tf_op jit(solution)/shard_map/sub | solution.py:60
  198.8 4.5 %fusion.5 = bf16[4,128,256]{2,1,0:T(8,128)(2,1)} fusion(f32[4,256]{1,0:T(4,128)S(1)} %exponential_reduce_fusion, bf16[1280,4,128]{2,1,0:T(4,128)(2,1)S(1)} %copy-done.1, bf16[256,4,128]{2,0,1:T(8,128)(2,1)} %pad_maximum_fusion.2, pred[256,1280]{1,0:T(8,128)(4,1)S(1)} %compare_and_fusion, bf16[1280,4,128]{2,1,0:T(4,128)(2,1)S(1)} %copy-done), kind=kOutput, calls=%fused_computation.10 | convolution fusion | flops 677775616 | bytes 3477504 | tf_op jit(solution)/shard_map/hqk,khd->qhd/dot_general | solution.py:62
  203.3 18.3 %all-to-all-done = bf16[4,512,1024]{2,1,0:T(8,128)(2,1)} async-done(((bf16[4,512,1024]{2,1,0:T(8,128)(2,1)}), bf16[4,512,1024]{2,1,0:T(8,128)(2,1)}, u32[]{:S(2)}, u32[]{:S(2)}) %all-to-all-start) | async-done | bytes 4194336 | tf_op jit(solution)/shard_map/all_to_all | solution.py:92
  221.6 6.2 %copy.76 = bf16[512,4,1024]{0,2,1:T(8,128)(2,1)} copy(bf16[512,4,1024]{2,0,1:T(8,128)(2,1)} %bitcast.18) | data formatting | bytes 8388608 | tf_op jit(solution)/shard_map/all_to_all | solution.py:92
  227.9 5.5 %fusion.32 = f32[256,4096]{1,0:T(8,128)} fusion(bf16[256,512]{0,1:T(8,128)(2,1)S(1)} %bitcast.53, bf16[512,4096]{0,1:T(8,128)(2,1)} %bitcast.42), kind=kOutput, calls=%fused_computation.56 | convolution fusion | flops 1073741824 | bytes 8650752 | tf_op jit(solution)/shard_map/dot_general | solution.py:95
  233.3 0.0 reduce-scatter.2.cloned.1.call-update
  233.3 0.0 copy-start.6
  233.4 0.1 reshape.215
  233.4 0.4 copy.78
  233.8 0.3 copy.79
  234.1 0.0 copy-start.5
  234.1 0.7 convolution_convert_fusion
  234.8 0.9 copy.80
  235.7 46.8 %reduce-scatter.2.cloned.1.call-done = f32[256,1024]{1,0:T(8,128)} async-done(((f32[256,4096]{1,0:T(8,128)}), f32[256,1024]{1,0:T(8,128)}) %reduce-scatter.2.cloned.1.call-update) | async-done | bytes 1048592 | tf_op jit(solution)/shard_map/reduce_scatter | solution.py:96
  282.5 2.1 add_convert_fusion
  (29 shorter events, 0.2 us)
Async XLA Ops:
  7.2 160.9 %all-gather.2.cloned.1.call-start = ((), (), s32[]{:S(2)}) async-start(), calls=%async_computation.2 | async-start | bytes 4227072 | tf_op jit(solution)/shard_map/all_gather | solution.py:91
  11.5 15.3 %copy-start.2 = (bf16[256,512]{1,0:T(8,128)(2,1)S(1)}, bf16[256,512]{1,0:T(8,128)(2,1)}, u32[]{:S(2)}) copy-start(bf16[256,512]{1,0:T(8,128)(2,1)} %param.9) | copy-start | bytes 786436
  11.6 20.6 %copy-start.4 = (bf16[256,512]{1,0:T(8,128)(2,1)S(1)}, bf16[256,512]{1,0:T(8,128)(2,1)}, u32[]{:S(2)}) copy-start(bf16[256,512]{1,0:T(8,128)(2,1)} %param.7) | copy-start | bytes 786436
  12.0 162.4 %collective-permute-start.4 = (bf16[256,512]{0,1:T(8,128)(2,1)S(1)}, bf16[256,512]{0,1:T(8,128)(2,1)}, u32[]{:S(2)}, u32[]{:S(2)}) collective-permute-start(bf16[256,512]{0,1:T(8,128)(2,1)S(1)} %bitcast.44), channel_id=1, source_target_pairs={{0,16},{4,20},{8,24},{12,28},{16,32},{20,36},{24,40},{28,44},{32,4... | collective-permute-start | bytes 786440 | tf_op jit(solution)/shard_map/ppermute | solution.py:19
  18.2 165.1 %collective-permute-start.5 = (bf16[256,512]{0,1:T(8,128)(2,1)S(1)}, bf16[256,512]{0,1:T(8,128)(2,1)}, u32[]{:S(2)}, u32[]{:S(2)}) collective-permute-start(bf16[256,512]{0,1:T(8,128)(2,1)S(1)} %bitcast.45), channel_id=1, source_target_pairs={{0,12},{4,16},{8,20},{12,24},{16,28},{20,32},{24,36},{28,40},{32,4... | collective-permute-start | bytes 786440 | tf_op jit(solution)/shard_map/ppermute | solution.py:19
  22.5 164.3 %collective-permute-start.6 = (bf16[256,512]{0,1:T(8,128)(2,1)S(1)}, bf16[256,512]{0,1:T(8,128)(2,1)S(1)}, u32[]{:S(2)}, u32[]{:S(2)}) collective-permute-start(bf16[256,512]{0,1:T(8,128)(2,1)S(1)} %bitcast.46), channel_id=1, source_target_pairs={{0,8},{4,12},{8,16},{12,20},{16,24},{20,28},{24,32},{28,36},{32,40... | collective-permute-start | bytes 786440 | tf_op jit(solution)/shard_map/ppermute | solution.py:19
  24.9 162.6 %collective-permute-start.7 = (bf16[256,512]{0,1:T(8,128)(2,1)S(1)}, bf16[256,512]{0,1:T(8,128)(2,1)S(1)}, u32[]{:S(2)}, u32[]{:S(2)}) collective-permute-start(bf16[256,512]{0,1:T(8,128)(2,1)S(1)} %bitcast.47), channel_id=1, source_target_pairs={{0,4},{4,8},{8,12},{12,16},{16,20},{20,24},{24,28},{28,32},{32,36}... | collective-permute-start | bytes 786440 | tf_op jit(solution)/shard_map/ppermute | solution.py:19
  26.9 152.9 %collective-permute-start = (bf16[256,512]{1,0:T(8,128)(2,1)S(1)}, bf16[256,512]{1,0:T(8,128)(2,1)}, u32[]{:S(2)}, u32[]{:S(2)}) collective-permute-start(bf16[256,512]{1,0:T(8,128)(2,1)S(1)} %copy-done.2), channel_id=1, source_target_pairs={{0,16},{4,20},{8,24},{12,28},{16,32},{20,36},{24,40},{28,44},{32,4... | collective-permute-start | bytes 786440 | tf_op jit(solution)/shard_map/ppermute | solution.py:19
  168.1 53.5 %all-to-all-start = ((bf16[4,512,1024]{2,1,0:T(8,128)(2,1)}), bf16[4,512,1024]{2,1,0:T(8,128)(2,1)}, u32[]{:S(2)}, u32[]{:S(2)}) async-start(bf16[4,512,1024]{2,1,0:T(8,128)(2,1)} %bitcast.43), calls=%async_computation | async-start | bytes 8388608 | tf_op jit(solution)/shard_map/all_to_all | solution.py:92
  172.9 109.6 %reduce-scatter.2.cloned.1.call-start = ((), (), s32[]{:S(2)}) async-start(), calls=%async_computation.3 | async-start | bytes 5242880 | tf_op jit(solution)/shard_map/reduce_scatter | solution.py:96
  174.4 14.0 %collective-permute-start.1 = (bf16[256,512]{1,0:T(8,128)(2,1)S(1)}, bf16[256,512]{1,0:T(8,128)(2,1)S(1)}, u32[]{:S(2)}, u32[]{:S(2)}) collective-permute-start(bf16[256,512]{1,0:T(8,128)(2,1)S(1)} %copy-done.2), channel_id=1, source_target_pairs={{0,12},{4,16},{8,20},{12,24},{16,28},{20,32},{24,36},{28,40},{32,4... | collective-permute-start | bytes 786440 | tf_op jit(solution)/shard_map/ppermute | solution.py:19
  179.7 12.2 %collective-permute-start.2 = (bf16[256,512]{1,0:T(8,128)(2,1)S(1)}, bf16[256,512]{1,0:T(8,128)(2,1)}, u32[]{:S(2)}, u32[]{:S(2)}) collective-permute-start(bf16[256,512]{1,0:T(8,128)(2,1)S(1)} %copy-done.2), channel_id=1, source_target_pairs={{0,8},{4,12},{8,16},{12,20},{16,24},{20,28},{24,32},{28,36},{32,40... | collective-permute-start | bytes 786440 | tf_op jit(solution)/shard_map/ppermute | solution.py:19
  183.2 9.7 %collective-permute-start.3 = (bf16[256,512]{1,0:T(8,128)(2,1)S(1)}, bf16[256,512]{1,0:T(8,128)(2,1)}, u32[]{:S(2)}, u32[]{:S(2)}) collective-permute-start(bf16[256,512]{1,0:T(8,128)(2,1)S(1)} %copy-done.2), channel_id=1, source_target_pairs={{0,4},{4,8},{8,12},{12,16},{16,20},{20,24},{24,28},{28,32},{32,36}... | collective-permute-start | bytes 786440 | tf_op jit(solution)/shard_map/ppermute | solution.py:19
  194.0 1.8 copy-start
  195.7 3.1 %copy-start.1 = (bf16[1280,4,128]{2,1,0:T(4,128)(2,1)S(1)}, bf16[1280,4,128]{2,1,0:T(4,128)(2,1)}, u32[]{:S(2)}) copy-start(bf16[1280,4,128]{2,1,0:T(4,128)(2,1)} %reshape.209) | copy-start | bytes 3932164
  221.6 6.2 %copy-start.3 = (bf16[4,128,256]{2,1,0:T(8,128)(2,1)S(1)}, bf16[4,128,256]{2,1,0:T(8,128)(2,1)}, u32[]{:S(2)}) copy-start(bf16[4,128,256]{2,1,0:T(8,128)(2,1)} %fusion.5) | copy-start | bytes 786436
  233.3 0.8 copy-start.6
  234.1 48.4 %copy-start.5 = (f32[1024]{0:T(1024)S(1)}, f32[1024]{0:T(1024)}, u32[]{:S(2)}) copy-start(f32[1024]{0:T(1024)} %param.13) | copy-start | bytes 12292
Sparse Core Ops, SparseCore 0:
  11.1 156.9 all-gather.1
  233.5 49.0 reduce-scatter.1
where the time goes:
time: 292 us; the launch traced here: 291 us
  waiting for transfers between devices  201 us (69%)
  starting transfers between devices  33.2 us (11%)
  local copies, waits for them, and re-layouts  24.1 us (8%)
  between operations  14.4 us (5%)
  matrix products  13.7 us (5%)
  other arithmetic  5.11 us (2%)
    all_gather x1, waiting for transfers between devices, local(): weight_all_rows = lax.all_gather(out_weight, 'req', axis=0, tiled=True)  135 us
    reduce_scatter x1, waiting for transfers between devices, local(): lax.psum_scatter(partial_value, 'head', scatter_dimension=1, tiled=True)  46.8 us
    ppermute x8, starting transfers between devices, passed_along(): return lax.ppermute(array, axis, pairs)  28.3 us
    all_to_all x1, waiting for transfers between devices, local(): lax.all_to_all(weight_all_rows, 'head', split_axis=0, concat_axis=1, tile...  18.3 us
    unnamed x27, local copies, waits for them, and re-layouts  10.7 us
    all_to_all x1, local copies, waits for them, and re-layouts, local(): lax.all_to_all(weight_all_rows, 'head', split_axis=0, concat_axis=1, tile...  6.23 us
  transfers between devices with their start and end apart: 11, of which 3 were waited for; matrix products, arithmetic and copies ran while one was open for 10% of the time, Pallas kernels for 0%

commit v1 on v0

--- a/solution.py
+++ b/solution.py
@@ -88,7 +88,9 @@
     key_id, key_position = request_info(lengths, key_tokens)
     mixed = attend_block(query_rot, key_all, value_all, request_id, own_tokens, key_id, key_tokens)
     heads_out = mixed.reshape(TOK_DEV, local_heads * DH)
-    weight_all_rows = lax.all_gather(out_weight, "req", axis=0, tiled=True)
+    weight_all_rows = jnp.concatenate(
+        lax.all_to_all(jnp.stack([out_weight] * lax.axis_size("req")), "req", 0, 0), axis=0
+    )
     weight_own_rows = lax.all_to_all(
         weight_all_rows, "head", split_axis=0, concat_axis=1, tiled=True
     )

time: 292 us -> 348 us (1.19)
  waiting for transfers between devices: 201 us -> 231 us
  starting transfers between devices: 33.2 us -> 57.3 us
    all_to_all x0 -> x1, waiting for transfers between devices: none -> 162 us  [local(): lax.all_to_all(jnp.stack([out_weight] * lax.axis_size('req')), 'req', 0, 0)]
    all_gather x1 -> x0, waiting for transfers between devices: 135 us -> none  [local(): weight_all_rows = lax.all_gather(out_weight, 'req', axis=0, tiled=True)]
    all_to_all x0 -> x1, starting transfers between devices: none -> 21 us  [local(): lax.all_to_all(jnp.stack([out_weight] * lax.axis_size('req')), 'req', 0, 0)]
    reduce_scatter x1, waiting for transfers between devices: 46.8 us -> 60.5 us  [local(): lax.psum_scatter(partial_value, 'head', scatter_dimension=1, tiled=True)]
    all_to_all x1, waiting for transfers between devices: 18.3 us -> 8.56 us  [local(): lax.all_to_all(weight_all_rows, 'head', split_axis=0, concat_axis=1, tile...]
    unnamed x27 -> x31, local copies, waits for them, and re-layouts: 10.7 us -> 9.83 us
  transfers between devices with their start and end apart: 11 -> 11, of which waited for: 3 -> 3; matrix products, arithmetic and copies ran while one was open for 10% -> 8% of each run, Pallas kernels for 0% -> 0%
where the time goes in v1:
time: 348 us; the launch traced here: 347 us
  waiting for transfers between devices  231 us (66%)
  starting transfers between devices  57.3 us (16%)
  local copies, waits for them, and re-layouts  25.8 us (7%)
  between operations  14.4 us (4%)
  matrix products  13.7 us (4%)
  other arithmetic  4.45 us (1%)
    all_to_all x1, waiting for transfers between devices, local(): lax.all_to_all(jnp.stack([out_weight] * lax.axis_size('req')), 'req', 0, 0)  162 us
    reduce_scatter x1, waiting for transfers between devices, local(): lax.psum_scatter(partial_value, 'head', scatter_dimension=1, tiled=True)  60.5 us
    ppermute x8, starting transfers between devices, passed_along(): return lax.ppermute(array, axis, pairs)  31.5 us
    all_to_all x1, starting transfers between devices, local(): lax.all_to_all(jnp.stack([out_weight] * lax.axis_size('req')), 'req', 0, 0)  21 us
    unnamed x31, local copies, waits for them, and re-layouts  9.83 us
    all_to_all x1, waiting for transfers between devices, local(): lax.all_to_all(weight_all_rows, 'head', split_axis=0, concat_axis=1, tile...  8.56 us
  transfers between devices with their start and end apart: 11, of which 3 were waited for; matrix products, arithmetic and copies ran while one was open for 8% of the time, Pallas kernels for 0%

profile of v1, /device:TPU:1, one launch (start us, length us, event | category | flops | bytes accessed | tf_op | source)
XLA Modules:
  0.0 346.8 jit_solution(11352651966477247437)
XLA Ops:
  7.2 3.3 stack.37
  10.4 21.0 %all-to-all-start = ((bf16[128,16,1024]{2,1,0:T(8,128)(2,1)}), bf16[128,16,1024]{2,1,0:T(8,128)(2,1)}, u32[]{:S(2)}, u32[]{:S(2)}) async-start(bf16[128,16,1024]{2,1,0:T(8,128)(2,1)} %stack.37), calls=%async_computation | async-start | bytes 8388608 | tf_op jit(solution)/shard_map/all_to_all | solution.py:92
  31.4 0.1 copy.62
  31.5 0.1 reduce-window.9
  31.6 0.1 multiply_reduce_fusion
  31.8 0.1 fusion.11
  31.9 0.1 multiply_cosine_fusion
  32.0 0.1 copy.65
  32.1 0.1 copy.66
  32.2 0.1 copy.68
  32.4 0.2 copy.84
  32.6 0.2 copy.85
  32.8 0.0 copy-start.2
  32.8 0.0 copy-start.5
  32.8 0.1 multiply_subtract_fusion
  33.0 0.1 copy.71
  33.1 0.1 copy.72
  33.3 5.5 %collective-permute-start.4 = (bf16[256,512]{0,1:T(8,128)(2,1)S(1)}, bf16[256,512]{0,1:T(8,128)(2,1)}, u32[]{:S(2)}, u32[]{:S(2)}) collective-permute-start(bf16[256,512]{0,1:T(8,128)(2,1)S(1)} %bitcast.43), channel_id=1, source_target_pairs={{0,16},{4,20},{8,24},{12,28},{16,32},{20,36},{24,40},{28,44},{32,4... | collective-permute-start | bytes 786440 | tf_op jit(solution)/shard_map/ppermute | solution.py:19
  38.7 3.7 %collective-permute-start.5 = (bf16[256,512]{0,1:T(8,128)(2,1)S(1)}, bf16[256,512]{0,1:T(8,128)(2,1)}, u32[]{:S(2)}, u32[]{:S(2)}) collective-permute-start(bf16[256,512]{0,1:T(8,128)(2,1)S(1)} %bitcast.44), channel_id=1, source_target_pairs={{0,12},{4,16},{8,20},{12,24},{16,28},{20,32},{24,36},{28,40},{32,4... | collective-permute-start | bytes 786440 | tf_op jit(solution)/shard_map/ppermute | solution.py:19
  42.4 2.4 collective-permute-start.6
  44.8 2.2 collective-permute-start.7
  47.0 5.0 %collective-permute-start = (bf16[256,512]{1,0:T(8,128)(2,1)S(1)}, bf16[256,512]{1,0:T(8,128)(2,1)}, u32[]{:S(2)}, u32[]{:S(2)}) collective-permute-start(bf16[256,512]{1,0:T(8,128)(2,1)S(1)} %copy-done.2), channel_id=1, source_target_pairs={{0,16},{4,20},{8,24},{12,28},{16,32},{20,36},{24,40},{28,44},{32,4... | collective-permute-start | bytes 786440 | tf_op jit(solution)/shard_map/ppermute | solution.py:19
  52.0 0.1 copy.63
  52.2 0.2 copy.64
  52.4 0.1 convert_reduce_fusion
  52.5 0.3 compare_and_fusion
  52.9 161.9 %all-to-all-done = bf16[128,16,1024]{2,1,0:T(8,128)(2,1)} async-done(((bf16[128,16,1024]{2,1,0:T(8,128)(2,1)}), bf16[128,16,1024]{2,1,0:T(8,128)(2,1)}, u32[]{:S(2)}, u32[]{:S(2)}) %all-to-all-start) | async-done | bytes 4194336 | tf_op jit(solution)/shard_map/all_to_all | solution.py:92
  214.8 4.8 %all-to-all-start.1 = ((bf16[4,512,1024]{2,1,0:T(8,128)(2,1)}), bf16[4,512,1024]{2,1,0:T(8,128)(2,1)}, u32[]{:S(2)}, u32[]{:S(2)}) async-start(bf16[4,512,1024]{2,1,0:T(8,128)(2,1)} %bitcast.17), calls=%async_computation.1 | async-start | bytes 8388608 | tf_op jit(solution)/shard_map/all_to_all | solution.py:94
  219.7 0.0 reduce-scatter.2.cloned.1.call-start
  219.7 0.3 subtract_convert_fusion
  220.0 0.1 slice.27
  220.1 1.0 pad_maximum_fusion.2
  221.1 0.0 collective-permute-done.4
  221.1 7.0 %collective-permute-start.1 = (bf16[256,512]{1,0:T(8,128)(2,1)S(1)}, bf16[256,512]{1,0:T(8,128)(2,1)S(1)}, u32[]{:S(2)}, u32[]{:S(2)}) collective-permute-start(bf16[256,512]{1,0:T(8,128)(2,1)S(1)} %copy-done.2), channel_id=1, source_target_pairs={{0,12},{4,16},{8,20},{12,24},{16,28},{20,32},{24,36},{28,40},{32,4... | collective-permute-start | bytes 786440 | tf_op jit(solution)/shard_map/ppermute | solution.py:19
  228.0 1.7 bitcast_dynamic-update-slice_fusion.3
  229.7 3.7 %collective-permute-start.2 = (bf16[256,512]{1,0:T(8,128)(2,1)S(1)}, bf16[256,512]{1,0:T(8,128)(2,1)}, u32[]{:S(2)}, u32[]{:S(2)}) collective-permute-start(bf16[256,512]{1,0:T(8,128)(2,1)S(1)} %copy-done.2), channel_id=1, source_target_pairs={{0,8},{4,12},{8,16},{12,20},{16,24},{20,28},{24,32},{28,36},{32,40... | collective-permute-start | bytes 786440 | tf_op jit(solution)/shard_map/ppermute | solution.py:19
  233.4 1.0 bitcast_dynamic-update-slice_fusion.8
  234.4 0.0 collective-permute-done.5
  234.4 2.1 collective-permute-start.3
  236.5 1.7 bitcast_dynamic-update-slice_fusion.2
  238.2 0.7 bitcast_dynamic-update-slice_fusion.1
  238.9 0.7 bitcast_dynamic-update-slice_fusion
  239.7 0.7 constant_dynamic-update-slice_fusion
  240.4 1.6 copy.73
  242.0 1.3 reshape.215
  243.3 1.0 bitcast_dynamic-update-slice_fusion.6
  244.3 1.0 bitcast_dynamic-update-slice_fusion.5
  245.3 1.3 reshape.213
  246.6 0.5 copy-done
  247.1 3.1 exponential_reduce_fusion
  250.2 4.5 %fusion.5 = bf16[4,128,256]{2,1,0:T(8,128)(2,1)} fusion(f32[4,256]{1,0:T(4,128)S(1)} %exponential_reduce_fusion, bf16[1280,4,128]{2,1,0:T(4,128)(2,1)S(1)} %copy-done.1, bf16[256,4,128]{2,0,1:T(8,128)(2,1)} %pad_maximum_fusion.2, pred[256,1280]{1,0:T(8,128)(4,1)S(1)} %compare_and_fusion, bf16[1280,4,128]{2,1,0:T(4,128)(2,1)S(1)} %copy-done), kind=kOutput, calls=%fused_computation.10 | convolution fusion | flops 677775616 | bytes 3477504 | tf_op jit(solution)/shard_map/hqk,khd->qhd/dot_general | solution.py:62
  254.6 8.6 %all-to-all-done.1 = bf16[4,512,1024]{2,1,0:T(8,128)(2,1)} async-done(((bf16[4,512,1024]{2,1,0:T(8,128)(2,1)}), bf16[4,512,1024]{2,1,0:T(8,128)(2,1)}, u32[]{:S(2)}, u32[]{:S(2)}) %all-to-all-start.1) | async-done | bytes 4194336 | tf_op jit(solution)/shard_map/all_to_all | solution.py:94
  263.2 6.3 %copy.76 = bf16[512,4,1024]{0,2,1:T(8,128)(2,1)} copy(bf16[512,4,1024]{2,0,1:T(8,128)(2,1)} %bitcast.18) | data formatting | bytes 8388608 | tf_op jit(solution)/shard_map/all_to_all | solution.py:94
  269.4 5.5 %fusion.32 = f32[256,4096]{1,0:T(8,128)} fusion(bf16[256,512]{0,1:T(8,128)(2,1)S(1)} %bitcast.52, bf16[512,4096]{0,1:T(8,128)(2,1)} %bitcast.42), kind=kOutput, calls=%fused_computation.56 | convolution fusion | flops 1073741824 | bytes 8650752 | tf_op jit(solution)/shard_map/dot_general | solution.py:97
  274.9 0.0 reduce-scatter.2.cloned.1.call-update
  274.9 0.0 copy-start.8
  275.0 0.1 reshape.219
  275.0 0.4 copy.78
  275.4 0.3 copy.79
  275.7 0.0 copy-start.6
  275.7 0.7 convolution_convert_fusion
  276.4 0.9 copy.80
  277.3 60.5 %reduce-scatter.2.cloned.1.call-done = f32[256,1024]{1,0:T(8,128)} async-done(((f32[256,4096]{1,0:T(8,128)}), f32[256,1024]{1,0:T(8,128)}) %reduce-scatter.2.cloned.1.call-update) | async-done | bytes 1048592 | tf_op jit(solution)/shard_map/reduce_scatter | solution.py:98
  337.8 2.1 add_convert_fusion
  (33 shorter events, 0.2 us)
Async XLA Ops:
  10.4 21.0 %copy-start.7 = (s32[64]{0:T(128)S(1)}, s32[64]{0:T(128)}, u32[]{:S(2)}) copy-start(s32[64]{0:T(128)} %param.10) | copy-start | bytes 772
  10.4 21.8 %copy-start.4 = (bf16[256,512]{1,0:T(8,128)(2,1)S(1)}, bf16[256,512]{1,0:T(8,128)(2,1)}, u32[]{:S(2)}) copy-start(bf16[256,512]{1,0:T(8,128)(2,1)} %param.8) | copy-start | bytes 786436
  10.4 204.4 %all-to-all-start = ((bf16[128,16,1024]{2,1,0:T(8,128)(2,1)}), bf16[128,16,1024]{2,1,0:T(8,128)(2,1)}, u32[]{:S(2)}, u32[]{:S(2)}) async-start(bf16[128,16,1024]{2,1,0:T(8,128)(2,1)} %stack.37), calls=%async_computation | async-start | bytes 8388608 | tf_op jit(solution)/shard_map/all_to_all | solution.py:92
  32.8 14.2 %copy-start.2 = (bf16[256,512]{1,0:T(8,128)(2,1)S(1)}, bf16[256,512]{1,0:T(8,128)(2,1)}, u32[]{:S(2)}) copy-start(bf16[256,512]{1,0:T(8,128)(2,1)} %param.9) | copy-start | bytes 786436
  32.8 19.2 %copy-start.5 = (bf16[256,512]{1,0:T(8,128)(2,1)S(1)}, bf16[256,512]{1,0:T(8,128)(2,1)}, u32[]{:S(2)}) copy-start(bf16[256,512]{1,0:T(8,128)(2,1)} %param.7) | copy-start | bytes 786436
  33.3 187.8 %collective-permute-start.4 = (bf16[256,512]{0,1:T(8,128)(2,1)S(1)}, bf16[256,512]{0,1:T(8,128)(2,1)}, u32[]{:S(2)}, u32[]{:S(2)}) collective-permute-start(bf16[256,512]{0,1:T(8,128)(2,1)S(1)} %bitcast.43), channel_id=1, source_target_pairs={{0,16},{4,20},{8,24},{12,28},{16,32},{20,36},{24,40},{28,44},{32,4... | collective-permute-start | bytes 786440 | tf_op jit(solution)/shard_map/ppermute | solution.py:19
  38.7 195.6 %collective-permute-start.5 = (bf16[256,512]{0,1:T(8,128)(2,1)S(1)}, bf16[256,512]{0,1:T(8,128)(2,1)}, u32[]{:S(2)}, u32[]{:S(2)}) collective-permute-start(bf16[256,512]{0,1:T(8,128)(2,1)S(1)} %bitcast.44), channel_id=1, source_target_pairs={{0,12},{4,16},{8,20},{12,24},{16,28},{20,32},{24,36},{28,40},{32,4... | collective-permute-start | bytes 786440 | tf_op jit(solution)/shard_map/ppermute | solution.py:19
  42.4 195.8 %collective-permute-start.6 = (bf16[256,512]{0,1:T(8,128)(2,1)S(1)}, bf16[256,512]{0,1:T(8,128)(2,1)S(1)}, u32[]{:S(2)}, u32[]{:S(2)}) collective-permute-start(bf16[256,512]{0,1:T(8,128)(2,1)S(1)} %bitcast.45), channel_id=1, source_target_pairs={{0,8},{4,12},{8,16},{12,20},{16,24},{20,28},{24,32},{28,36},{32,40... | collective-permute-start | bytes 786440 | tf_op jit(solution)/shard_map/ppermute | solution.py:19
  44.8 194.1 %collective-permute-start.7 = (bf16[256,512]{0,1:T(8,128)(2,1)S(1)}, bf16[256,512]{0,1:T(8,128)(2,1)S(1)}, u32[]{:S(2)}, u32[]{:S(2)}) collective-permute-start(bf16[256,512]{0,1:T(8,128)(2,1)S(1)} %bitcast.46), channel_id=1, source_target_pairs={{0,4},{4,8},{8,12},{12,16},{16,20},{20,24},{24,28},{28,32},{32,36}... | collective-permute-start | bytes 786440 | tf_op jit(solution)/shard_map/ppermute | solution.py:19
  47.0 182.7 %collective-permute-start = (bf16[256,512]{1,0:T(8,128)(2,1)S(1)}, bf16[256,512]{1,0:T(8,128)(2,1)}, u32[]{:S(2)}, u32[]{:S(2)}) collective-permute-start(bf16[256,512]{1,0:T(8,128)(2,1)S(1)} %copy-done.2), channel_id=1, source_target_pairs={{0,16},{4,20},{8,24},{12,28},{16,32},{20,36},{24,40},{28,44},{32,4... | collective-permute-start | bytes 786440 | tf_op jit(solution)/shard_map/ppermute | solution.py:19
  214.8 48.4 %all-to-all-start.1 = ((bf16[4,512,1024]{2,1,0:T(8,128)(2,1)}), bf16[4,512,1024]{2,1,0:T(8,128)(2,1)}, u32[]{:S(2)}, u32[]{:S(2)}) async-start(bf16[4,512,1024]{2,1,0:T(8,128)(2,1)} %bitcast.17), calls=%async_computation.1 | async-start | bytes 8388608 | tf_op jit(solution)/shard_map/all_to_all | solution.py:94
  219.7 118.2 %reduce-scatter.2.cloned.1.call-start = ((), (), s32[]{:S(2)}) async-start(), calls=%async_computation.3 | async-start | bytes 5242880 | tf_op jit(solution)/shard_map/reduce_scatter | solution.py:98
  221.1 18.6 %collective-permute-start.1 = (bf16[256,512]{1,0:T(8,128)(2,1)S(1)}, bf16[256,512]{1,0:T(8,128)(2,1)S(1)}, u32[]{:S(2)}, u32[]{:S(2)}) collective-permute-start(bf16[256,512]{1,0:T(8,128)(2,1)S(1)} %copy-done.2), channel_id=1, source_target_pairs={{0,12},{4,16},{8,20},{12,24},{16,28},{20,32},{24,36},{28,40},{32,4... | collective-permute-start | bytes 786440 | tf_op jit(solution)/shard_map/ppermute | solution.py:19
  229.7 13.6 %collective-permute-start.2 = (bf16[256,512]{1,0:T(8,128)(2,1)S(1)}, bf16[256,512]{1,0:T(8,128)(2,1)}, u32[]{:S(2)}, u32[]{:S(2)}) collective-permute-start(bf16[256,512]{1,0:T(8,128)(2,1)S(1)} %copy-done.2), channel_id=1, source_target_pairs={{0,8},{4,12},{8,16},{12,20},{16,24},{20,28},{24,32},{28,36},{32,40... | collective-permute-start | bytes 786440 | tf_op jit(solution)/shard_map/ppermute | solution.py:19
  234.4 9.9 %collective-permute-start.3 = (bf16[256,512]{1,0:T(8,128)(2,1)S(1)}, bf16[256,512]{1,0:T(8,128)(2,1)}, u32[]{:S(2)}, u32[]{:S(2)}) collective-permute-start(bf16[256,512]{1,0:T(8,128)(2,1)S(1)} %copy-done.2), channel_id=1, source_target_pairs={{0,4},{4,8},{8,12},{12,16},{16,20},{20,24},{24,28},{28,32},{32,36}... | collective-permute-start | bytes 786440 | tf_op jit(solution)/shard_map/ppermute | solution.py:19
  245.3 1.8 copy-start
  247.1 3.1 copy-start.1
  263.2 6.3 %copy-start.3 = (bf16[4,128,256]{2,1,0:T(8,128)(2,1)S(1)}, bf16[4,128,256]{2,1,0:T(8,128)(2,1)}, u32[]{:S(2)}) copy-start(bf16[4,128,256]{2,1,0:T(8,128)(2,1)} %fusion.5) | copy-start | bytes 786436
  274.9 0.8 copy-start.8
  275.7 62.1 %copy-start.6 = (f32[1024]{0:T(1024)S(1)}, f32[1024]{0:T(1024)}, u32[]{:S(2)}) copy-start(f32[1024]{0:T(1024)} %param.13) | copy-start | bytes 12292
Sparse Core Ops, SparseCore 0:
  275.1 62.7 reduce-scatter.1
